TPU v7x, 256 devices: a whole 4x4x8 slice. The times are simulated.
256 devices in a mesh: seq: 16 (over x_hi, z), row: 4 (over x_lo, core), col: 4 (over y).
Axes of the slice: x: 4 (x_hi: 2, x_lo: 2; x = x_hi * 2 + x_lo), y: 4, z: 8, core: 2. Of those that a mesh axis runs over, the one named last changes fastest.
Arguments:
- tokens: bfloat16 [8192, 4096], P(('seq', 'col'), 'row'), may hold values from -11 to 11
- w_query: bfloat16 [4096, 4096], P('row', 'col'), as said below
- w_key: bfloat16 [4096, 1024], P('row', 'col'), as said below
- w_value: bfloat16 [4096, 1024], P('row', 'col'), may hold values from -0.09375 to 0.09375
- w_output: bfloat16 [4096, 4096], P('col', 'row'), may hold values from -0.09375 to 0.09375
Outputs:
- attended: bfloat16 [8192, 4096], P(('seq', 'col'), 'row')
Inputs may be any that keep to these rules, and one draw needn't show every extreme that they name: `w_query`: entries below 6 / sqrt(4096) in magnitude. `w_key`: entries below 8.4 / sqrt(4096) in magnitude.
All inputs are finite; a program needn't handle non-finite values.
Results may differ from a plain program's by a relative error of at most 0.025.
Values may be sent and summed in bfloat16 or wider, within the bound.
No kernel may reach another device: no remote copies, remote signals or barrier semaphores. Data moves between devices by JAX's collectives and lax.ppermute only.
A program may use at most 64 MiB of HBM per device.

v0:
```python
import jax
import jax.numpy as jnp
from jax import lax
from jax.sharding import PartitionSpec as P

HEADS = 32
KV_HEADS = 8
HEAD_DIM = 128
rope_base = 500000.0
masked_score = -1e30


def passed_along(value, axis, steps):
    count = lax.axis_size(axis)
    initial, last = (max(0, -steps), min(count, count - steps))
    return lax.ppermute(value, axis, [(source, source + steps) for source in range(initial, last)])


def rotate(values, positions):
    half = HEAD_DIM // 2
    freqs = rope_base ** (-(jnp.arange(half, dtype=jnp.float32) * 2.0) / HEAD_DIM)
    angles = positions.astype(jnp.float32)[:, None] * freqs[None, :]
    cosine = jnp.concatenate([jnp.cos(angles), jnp.cos(angles)], axis=1)
    sine = jnp.concatenate([jnp.sin(angles), jnp.sin(angles)], axis=1)
    count = values.shape[0]
    heads = values.reshape(count, -1, HEAD_DIM)
    turned = jnp.concatenate([-heads[..., half:], heads[..., :half]], axis=-1)
    result = heads * cosine[:, None, :] + turned * sine[:, None, :]
    return result.reshape(count, -1)


def on_device(tokens, w_query, w_key, w_value, w_output):
    shard_rows = tokens.shape[0]
    col_count = lax.axis_size("col")
    row_count = lax.axis_size("row")
    seq_count = lax.axis_size("seq")
    rows_dev = shard_rows * col_count // row_count
    block_len = rows_dev * row_count
    seq_at = lax.axis_index("seq")
    row_at = lax.axis_index("row")
    width_q = w_query.shape[1]
    width_kv = w_key.shape[1]
    local_kv = width_kv // HEAD_DIM
    group = HEADS // KV_HEADS
    score_scale = HEAD_DIM ** (-0.5)
    local_index = jnp.arange(block_len, dtype=jnp.int32)
    gathered_block = lax.all_gather(tokens, "col", axis=0, tiled=True)
    block_pos = seq_at * block_len + local_index
    regrouped = lax.all_to_all(gathered_block, "row", split_axis=0, concat_axis=1, tiled=True)
    projected = jnp.concatenate(
        [
            jnp.dot(
                regrouped,
                lax.all_gather(w_query, "row", axis=0, tiled=True),
                preferred_element_type=jnp.float32,
            ),
            jnp.dot(
                regrouped,
                lax.all_gather(w_key, "row", axis=0, tiled=True),
                preferred_element_type=jnp.float32,
            ),
            jnp.dot(
                regrouped,
                lax.all_gather(w_value, "row", axis=0, tiled=True),
                preferred_element_type=jnp.float32,
            ),
        ],
        axis=1,
    )
    q_pos = lax.dynamic_slice_in_dim(block_pos, row_at * rows_dev, rows_dev, 0)
    query = rotate(projected[:, :width_q], q_pos).astype(jnp.bfloat16)
    key_rot = rotate(projected[:, width_q : width_q + width_kv], q_pos)
    kv_slab = jnp.concatenate([key_rot, projected[:, width_q + width_kv :]], axis=1).astype(
        jnp.bfloat16
    )
    query_grouped = query.reshape(rows_dev, local_kv, group, HEAD_DIM)
    diagonal_mask = block_pos[None, :] <= q_pos[:, None]

    def attend(carry_state, queries, kv_rows, allowed):
        peak, total, summed = carry_state
        count = kv_rows.shape[0]
        key_blk = kv_rows[:, :width_kv].reshape(count, local_kv, HEAD_DIM)
        value_blk = kv_rows[:, width_kv:].reshape(count, local_kv, HEAD_DIM)
        scores = (
            jnp.einsum("qgha,kga->ghqk", queries, key_blk, preferred_element_type=jnp.float32)
            * score_scale
        )
        if allowed is not None:
            scores = jnp.where(allowed, scores, masked_score)
        new_peak = jnp.maximum(peak, jnp.max(scores, axis=-1))
        weights = jnp.exp(scores - new_peak[..., None])
        factor = jnp.exp(peak - new_peak)
        total = total * factor + jnp.sum(weights, axis=-1)
        summed = summed * factor[..., None] + jnp.einsum(
            "ghqk,kga->ghqa",
            weights.astype(jnp.bfloat16),
            value_blk,
            preferred_element_type=jnp.float32,
        )
        return (new_peak, total, summed)

    start_state = (
        jnp.full((local_kv, group, rows_dev), masked_score, jnp.float32),
        jnp.zeros((local_kv, group, rows_dev), jnp.float32),
        jnp.zeros((local_kv, group, rows_dev, HEAD_DIM), jnp.float32),
    )

    def keep_state(carry_state):
        return carry_state

    def cycle_work(step_index, carry_state, kv_whole):
        source_dev = (seq_at - step_index) % seq_count
        return lax.cond(
            source_dev < seq_at,
            lambda inner: attend(inner, query_grouped, kv_whole, None),
            keep_state,
            carry_state,
        )

    kv_first = lax.all_gather(kv_slab, "row", axis=0, tiled=True)
    first_state = attend(start_state, query_grouped, kv_first, diagonal_mask)

    def cycle_turn(step_index, carry):
        carry_state, kv_here = carry
        kv_here = passed_along(kv_here, "seq", 1)
        return (cycle_work(step_index, carry_state, kv_here), kv_here)

    final_state, _ = lax.fori_loop(1, seq_count, cycle_turn, (first_state, kv_first))
    heads_sum = final_state[2] / final_state[1][..., None]
    heads_out = heads_sum.transpose(2, 0, 1, 3).reshape(rows_dev, width_q).astype(jnp.bfloat16)
    heads_block = lax.all_gather(heads_out, "row", axis=0, tiled=True)
    return lax.psum_scatter(
        jnp.dot(heads_block, w_output, preferred_element_type=jnp.float32).astype(jnp.bfloat16),
        "col",
        scatter_dimension=0,
        tiled=True,
    )


def solution(mesh):
    return jax.shard_map(
        on_device,
        mesh=mesh,
        in_specs=(
            P(("seq", "col"), "row"),
            P("row", "col"),
            P("row", "col"),
            P("row", "col"),
            P("col", "row"),
        ),
        out_specs=P(("seq", "col"), "row"),
        check_vma=False,
    )
```

profile of v0, /device:TPU:2, one launch (start us, length us, event | category | flops | bytes accessed | tf_op | source)
XLA Modules:
  0.0 549.9 jit_solution(10497414819965394275)
XLA Ops:
  9.3 29.5 %all-gather.6.cloned.1.call-done = bf16[512,1024]{1,0:T(8,128)(2,1)} async-done(((bf16[128,1024]{1,0:T(8,128)(2,1)}), bf16[512,1024]{1,0:T(8,128)(2,1)}) %all-gather.6.cloned.1.call-update) | async-done | bytes 1048592 | tf_op jit(solution)/shard_map/all_gather | solution.py:47
  38.8 4.0 all-to-all-start
  43.9 12.4 %all-to-all-done = bf16[4,128,1024]{2,1,0:T(8,128)(2,1)S(1)} async-done(((bf16[4,128,1024]{2,1,0:T(8,128)(2,1)}), bf16[4,128,1024]{2,1,0:T(8,128)(2,1)S(1)}, u32[]{:S(2)}, u32[]{:S(2)}) %all-to-all-start) | async-done | bytes 1048608 | tf_op jit(solution)/shard_map/all_to_all | solution.py:49
  61.0 2.4 copy.59
  63.3 9.0 %all-gather.8.cloned.1.call-done = bf16[4096,256]{1,0:T(8,128)(2,1)} async-done(((bf16[1024,256]{1,0:T(8,128)(2,1)}), bf16[4096,256]{1,0:T(8,128)(2,1)}) %all-gather.8.cloned.1.call-update) | async-done | bytes 2097168 | tf_op jit(solution)/shard_map/all_gather | solution.py:59
  72.3 4.1 copy.34
  76.4 2.3 fusion.22
  78.9 26.6 %all-gather.10.cloned.1.call-done = bf16[4096,256]{1,0:T(8,128)(2,1)} async-done(((bf16[1024,256]{1,0:T(8,128)(2,1)}), bf16[4096,256]{1,0:T(8,128)(2,1)}) %all-gather.10.cloned.1.call-update) | async-done | bytes 2097168 | tf_op jit(solution)/shard_map/all_gather | solution.py:64
  105.5 2.4 convolution_convert_fusion.1
  107.9 8.2 %all_gather.21 = bf16[512,512]{1,0:T(8,128)(2,1)} all-gather(bf16[128,512]{1,0:T(8,128)(2,1)S(1)} %pad_maximum_fusion), channel_id=1, replica_groups=mesh['seq'=16,'row'=4,'col'=4] {'row'}, dimensions={0}, use_global_device_ids=true | all-gather | bytes 655360 | tf_op jit(solution)/shard_map/all_gather | solution.py:120
  116.1 2.0 copy.41
  122.4 69.7 %all-gather.12.cloned.1.call-done = bf16[4096,1024]{1,0:T(8,128)(2,1)} async-done(((bf16[1024,1024]{1,0:T(8,128)(2,1)}), bf16[4096,1024]{1,0:T(8,128)(2,1)}) %all-gather.12.cloned.1.call-update) | async-done | bytes 8388624 | tf_op jit(solution)/shard_map/all_gather | solution.py:54
  192.1 11.6 %copy.36 = bf16[1024,4096]{1,0:T(8,128)(2,1)} copy(bf16[1024,4096]{0,1:T(8,128)(2,1)} %bitcast.60) | data formatting | bytes 16777216 | tf_op jit(solution)/shard_map/dot_general | solution.py:52
  203.7 5.7 %fusion.23 = f32[128,8,128]{0,2,1:T(8,128)S(1)} fusion(bf16[128,4096,1]{1,0,2:T(8,128)(2,1)S(1)} %reshape.59, bf16[8,128,4096]{2,1,0:T(8,128)(2,1)} %bitcast.55), kind=kOutput, calls=%fused_computation.46 | convolution fusion | flops 1073741824 | bytes 9961472 | tf_op jit(solution)/shard_map/dot_general | solution.py:52
  211.9 231.9 %while.21 = (s32[]{:T(128)}, f32[2,4,128]{2,1,0:T(4,128)S(1)}, f32[2,4,128]{2,1,0:T(4,128)S(1)}, f32[2,4,128,128]{3,2,1,0:T(8,128)S(1)}, bf16[512,512]{0,1:T(8,1...) while((s32[]{:T(128)}, f32[2,4,128]{2,1,0:T(4,128)S(1)}, ...), condition=%wide.region_7.8_spmd, body=%wide.region_2.7_spmd.sunk | while | flops 272893952 | bytes 12386684 | solution.py:128
  212.0 3.5 collective-permute-start
  215.5 12.5 %collective-permute-done = bf16[512,512]{0,1:T(8,128)(2,1)S(1)} collective-permute-done((bf16[512,512]{0,1:T(8,128)(2,1)}, bf16[512,512]{0,1:T(8,128)(2,1)S(1)}, u32[]{:S(2)}, u32[]{:S(2)}) %collective-permute-start) | collective-permute-done | bytes 524320 | tf_op jit(solution)/shard_map/while/body/eval_jaxpr/ppermute | solution.py:16
  228.8 6.0 %collective-permute-start = (bf16[512,512]{0,1:T(8,128)(2,1)}, bf16[512,512]{0,1:T(8,128)(2,1)S(1)}, u32[]{:S(2)}, u32[]{:S(2)}) collective-permute-start(bf16[512,512]{0,1:T(8,128)(2,1)} %get-tuple-element.353), channel_id=1, source_target_pairs={{0,16},{16,32},{32,48},{48,64},{64,80},{80,96},{96,112},{112,128},... | collective-permute-start | bytes 1572872 | tf_op jit(solution)/shard_map/while/body/eval_jaxpr/ppermute | solution.py:16
  234.8 11.7 %collective-permute-done = bf16[512,512]{0,1:T(8,128)(2,1)S(1)} collective-permute-done((bf16[512,512]{0,1:T(8,128)(2,1)}, bf16[512,512]{0,1:T(8,128)(2,1)S(1)}, u32[]{:S(2)}, u32[]{:S(2)}) %collective-permute-start) | collective-permute-done | bytes 524320 | tf_op jit(solution)/shard_map/while/body/eval_jaxpr/ppermute | solution.py:16
  247.3 4.3 collective-permute-start
  251.6 10.9 %collective-permute-done = bf16[512,512]{0,1:T(8,128)(2,1)S(1)} collective-permute-done((bf16[512,512]{0,1:T(8,128)(2,1)}, bf16[512,512]{0,1:T(8,128)(2,1)S(1)}, u32[]{:S(2)}, u32[]{:S(2)}) %collective-permute-start) | collective-permute-done | bytes 524320 | tf_op jit(solution)/shard_map/while/body/eval_jaxpr/ppermute | solution.py:16
  263.3 5.2 collective-permute-start
  268.5 10.0 %collective-permute-done = bf16[512,512]{0,1:T(8,128)(2,1)S(1)} collective-permute-done((bf16[512,512]{0,1:T(8,128)(2,1)}, bf16[512,512]{0,1:T(8,128)(2,1)S(1)}, u32[]{:S(2)}, u32[]{:S(2)}) %collective-permute-start) | collective-permute-done | bytes 524320 | tf_op jit(solution)/shard_map/while/body/eval_jaxpr/ppermute | solution.py:16
  279.3 5.1 collective-permute-start
  284.4 9.1 %collective-permute-done = bf16[512,512]{0,1:T(8,128)(2,1)S(1)} collective-permute-done((bf16[512,512]{0,1:T(8,128)(2,1)}, bf16[512,512]{0,1:T(8,128)(2,1)S(1)}, u32[]{:S(2)}, u32[]{:S(2)}) %collective-permute-start) | collective-permute-done | bytes 524320 | tf_op jit(solution)/shard_map/while/body/eval_jaxpr/ppermute | solution.py:16
  294.3 7.2 %collective-permute-start = (bf16[512,512]{0,1:T(8,128)(2,1)}, bf16[512,512]{0,1:T(8,128)(2,1)S(1)}, u32[]{:S(2)}, u32[]{:S(2)}) collective-permute-start(bf16[512,512]{0,1:T(8,128)(2,1)} %get-tuple-element.353), channel_id=1, source_target_pairs={{0,16},{16,32},{32,48},{48,64},{64,80},{80,96},{96,112},{112,128},... | collective-permute-start | bytes 1572872 | tf_op jit(solution)/shard_map/while/body/eval_jaxpr/ppermute | solution.py:16
  301.6 8.3 %collective-permute-done = bf16[512,512]{0,1:T(8,128)(2,1)S(1)} collective-permute-done((bf16[512,512]{0,1:T(8,128)(2,1)}, bf16[512,512]{0,1:T(8,128)(2,1)S(1)}, u32[]{:S(2)}, u32[]{:S(2)}) %collective-permute-start) | collective-permute-done | bytes 524320 | tf_op jit(solution)/shard_map/while/body/eval_jaxpr/ppermute | solution.py:16
  310.6 5.5 %collective-permute-start = (bf16[512,512]{0,1:T(8,128)(2,1)}, bf16[512,512]{0,1:T(8,128)(2,1)S(1)}, u32[]{:S(2)}, u32[]{:S(2)}) collective-permute-start(bf16[512,512]{0,1:T(8,128)(2,1)} %get-tuple-element.353), channel_id=1, source_target_pairs={{0,16},{16,32},{32,48},{48,64},{64,80},{80,96},{96,112},{112,128},... | collective-permute-start | bytes 1572872 | tf_op jit(solution)/shard_map/while/body/eval_jaxpr/ppermute | solution.py:16
  316.2 7.4 %collective-permute-done = bf16[512,512]{0,1:T(8,128)(2,1)S(1)} collective-permute-done((bf16[512,512]{0,1:T(8,128)(2,1)}, bf16[512,512]{0,1:T(8,128)(2,1)S(1)}, u32[]{:S(2)}, u32[]{:S(2)}) %collective-permute-start) | collective-permute-done | bytes 524320 | tf_op jit(solution)/shard_map/while/body/eval_jaxpr/ppermute | solution.py:16
  324.4 7.2 %collective-permute-start = (bf16[512,512]{0,1:T(8,128)(2,1)}, bf16[512,512]{0,1:T(8,128)(2,1)S(1)}, u32[]{:S(2)}, u32[]{:S(2)}) collective-permute-start(bf16[512,512]{0,1:T(8,128)(2,1)} %get-tuple-element.353), channel_id=1, source_target_pairs={{0,16},{16,32},{32,48},{48,64},{64,80},{80,96},{96,112},{112,128},... | collective-permute-start | bytes 1572872 | tf_op jit(solution)/shard_map/while/body/eval_jaxpr/ppermute | solution.py:16
  331.7 6.9 %collective-permute-done = bf16[512,512]{0,1:T(8,128)(2,1)S(1)} collective-permute-done((bf16[512,512]{0,1:T(8,128)(2,1)}, bf16[512,512]{0,1:T(8,128)(2,1)S(1)}, u32[]{:S(2)}, u32[]{:S(2)}) %collective-permute-start) | collective-permute-done | bytes 524320 | tf_op jit(solution)/shard_map/while/body/eval_jaxpr/ppermute | solution.py:16
  339.4 5.5 %collective-permute-start = (bf16[512,512]{0,1:T(8,128)(2,1)}, bf16[512,512]{0,1:T(8,128)(2,1)S(1)}, u32[]{:S(2)}, u32[]{:S(2)}) collective-permute-start(bf16[512,512]{0,1:T(8,128)(2,1)} %get-tuple-element.353), channel_id=1, source_target_pairs={{0,16},{16,32},{32,48},{48,64},{64,80},{80,96},{96,112},{112,128},... | collective-permute-start | bytes 1572872 | tf_op jit(solution)/shard_map/while/body/eval_jaxpr/ppermute | solution.py:16
  345.0 7.0 %collective-permute-done = bf16[512,512]{0,1:T(8,128)(2,1)S(1)} collective-permute-done((bf16[512,512]{0,1:T(8,128)(2,1)}, bf16[512,512]{0,1:T(8,128)(2,1)S(1)}, u32[]{:S(2)}, u32[]{:S(2)}) %collective-permute-start) | collective-permute-done | bytes 524320 | tf_op jit(solution)/shard_map/while/body/eval_jaxpr/ppermute | solution.py:16
  352.7 5.5 %collective-permute-start = (bf16[512,512]{0,1:T(8,128)(2,1)}, bf16[512,512]{0,1:T(8,128)(2,1)S(1)}, u32[]{:S(2)}, u32[]{:S(2)}) collective-permute-start(bf16[512,512]{0,1:T(8,128)(2,1)} %get-tuple-element.353), channel_id=1, source_target_pairs={{0,16},{16,32},{32,48},{48,64},{64,80},{80,96},{96,112},{112,128},... | collective-permute-start | bytes 1572872 | tf_op jit(solution)/shard_map/while/body/eval_jaxpr/ppermute | solution.py:16
  358.3 7.8 %collective-permute-done = bf16[512,512]{0,1:T(8,128)(2,1)S(1)} collective-permute-done((bf16[512,512]{0,1:T(8,128)(2,1)}, bf16[512,512]{0,1:T(8,128)(2,1)S(1)}, u32[]{:S(2)}, u32[]{:S(2)}) %collective-permute-start) | collective-permute-done | bytes 524320 | tf_op jit(solution)/shard_map/while/body/eval_jaxpr/ppermute | solution.py:16
  366.9 4.6 collective-permute-start
  371.5 6.9 %collective-permute-done = bf16[512,512]{0,1:T(8,128)(2,1)S(1)} collective-permute-done((bf16[512,512]{0,1:T(8,128)(2,1)}, bf16[512,512]{0,1:T(8,128)(2,1)S(1)}, u32[]{:S(2)}, u32[]{:S(2)}) %collective-permute-start) | collective-permute-done | bytes 524320 | tf_op jit(solution)/shard_map/while/body/eval_jaxpr/ppermute | solution.py:16
  379.3 7.7 %collective-permute-start = (bf16[512,512]{0,1:T(8,128)(2,1)}, bf16[512,512]{0,1:T(8,128)(2,1)S(1)}, u32[]{:S(2)}, u32[]{:S(2)}) collective-permute-start(bf16[512,512]{0,1:T(8,128)(2,1)} %get-tuple-element.353), channel_id=1, source_target_pairs={{0,16},{16,32},{32,48},{48,64},{64,80},{80,96},{96,112},{112,128},... | collective-permute-start | bytes 1572872 | tf_op jit(solution)/shard_map/while/body/eval_jaxpr/ppermute | solution.py:16
  387.0 7.1 %collective-permute-done = bf16[512,512]{0,1:T(8,128)(2,1)S(1)} collective-permute-done((bf16[512,512]{0,1:T(8,128)(2,1)}, bf16[512,512]{0,1:T(8,128)(2,1)S(1)}, u32[]{:S(2)}, u32[]{:S(2)}) %collective-permute-start) | collective-permute-done | bytes 524320 | tf_op jit(solution)/shard_map/while/body/eval_jaxpr/ppermute | solution.py:16
  394.9 7.7 %collective-permute-start = (bf16[512,512]{0,1:T(8,128)(2,1)}, bf16[512,512]{0,1:T(8,128)(2,1)S(1)}, u32[]{:S(2)}, u32[]{:S(2)}) collective-permute-start(bf16[512,512]{0,1:T(8,128)(2,1)} %get-tuple-element.353), channel_id=1, source_target_pairs={{0,16},{16,32},{32,48},{48,64},{64,80},{80,96},{96,112},{112,128},... | collective-permute-start | bytes 1572872 | tf_op jit(solution)/shard_map/while/body/eval_jaxpr/ppermute | solution.py:16
  402.6 6.9 %collective-permute-done = bf16[512,512]{0,1:T(8,128)(2,1)S(1)} collective-permute-done((bf16[512,512]{0,1:T(8,128)(2,1)}, bf16[512,512]{0,1:T(8,128)(2,1)S(1)}, u32[]{:S(2)}, u32[]{:S(2)}) %collective-permute-start) | collective-permute-done | bytes 524320 | tf_op jit(solution)/shard_map/while/body/eval_jaxpr/ppermute | solution.py:16
  410.4 10.7 %collective-permute-start = (bf16[512,512]{0,1:T(8,128)(2,1)}, bf16[512,512]{0,1:T(8,128)(2,1)S(1)}, u32[]{:S(2)}, u32[]{:S(2)}) collective-permute-start(bf16[512,512]{0,1:T(8,128)(2,1)} %get-tuple-element.353), channel_id=1, source_target_pairs={{0,16},{16,32},{32,48},{48,64},{64,80},{80,96},{96,112},{112,128},... | collective-permute-start | bytes 1572872 | tf_op jit(solution)/shard_map/while/body/eval_jaxpr/ppermute | solution.py:16
  421.1 8.8 %collective-permute-done = bf16[512,512]{0,1:T(8,128)(2,1)S(1)} collective-permute-done((bf16[512,512]{0,1:T(8,128)(2,1)}, bf16[512,512]{0,1:T(8,128)(2,1)S(1)}, u32[]{:S(2)}, u32[]{:S(2)}) %collective-permute-start) | collective-permute-done | bytes 524320 | tf_op jit(solution)/shard_map/while/body/eval_jaxpr/ppermute | solution.py:16
  430.7 5.4 collective-permute-start
  436.1 6.9 %collective-permute-done = bf16[512,512]{0,1:T(8,128)(2,1)S(1)} collective-permute-done((bf16[512,512]{0,1:T(8,128)(2,1)}, bf16[512,512]{0,1:T(8,128)(2,1)S(1)}, u32[]{:S(2)}, u32[]{:S(2)}) %collective-permute-start) | collective-permute-done | bytes 524320 | tf_op jit(solution)/shard_map/while/body/eval_jaxpr/ppermute | solution.py:16
  444.9 66.5 %all-gather.14.cloned.1.call-done = bf16[512,1024]{0,1:T(8,128)(2,1)} async-done(((bf16[128,1024]{0,1:T(8,128)(2,1)}), bf16[512,1024]{0,1:T(8,128)(2,1)}) %all-gather.14.cloned.1.call-update) | async-done | bytes 1048592 | tf_op jit(solution)/shard_map/all_gather | solution.py:131
  511.4 3.5 convolution_convert_fusion
  514.9 28.2 %reduce-scatter.2.cloned.1.call-done = bf16[128,1024]{1,0:T(8,128)(2,1)} async-done(((bf16[512,1024]{1,0:T(8,128)(2,1)}), bf16[128,1024]{1,0:T(8,128)(2,1)}) %reduce-scatter.2.cloned.1.call-update) | async-done | bytes 262160 | tf_op jit(solution)/shard_map/reduce_scatter | solution.py:132
  (77 shorter events, 28.3 us)
Async XLA Ops:
  6.5 504.9 %copy-start = (bf16[1024,1024]{1,0:T(8,128)(2,1)S(1)}, bf16[1024,1024]{1,0:T(8,128)(2,1)}, u32[]{:S(2)}) copy-start(bf16[1024,1024]{1,0:T(8,128)(2,1)} %param.13) | copy-start | bytes 6291460
  6.5 32.3 %all-gather.6.cloned.1.call-start = ((), (), s32[]{:S(2)}) async-start(), calls=%async_computation.2 | async-start | bytes 1310720 | tf_op jit(solution)/shard_map/all_gather | solution.py:47
  7.3 65.1 %all-gather.8.cloned.1.call-start = ((), (), s32[]{:S(2)}) async-start(), calls=%async_computation.3 | async-start | bytes 2621440 | tf_op jit(solution)/shard_map/all_gather | solution.py:59
  8.0 97.5 %all-gather.10.cloned.1.call-start = ((), (), s32[]{:S(2)}) async-start(), calls=%async_computation.4 | async-start | bytes 2621440 | tf_op jit(solution)/shard_map/all_gather | solution.py:64
  8.7 183.3 %all-gather.12.cloned.1.call-start = ((), (), s32[]{:S(2)}) async-start(), calls=%async_computation.5 | async-start | bytes 10485760 | tf_op jit(solution)/shard_map/all_gather | solution.py:54
  38.8 17.5 %all-to-all-start = ((bf16[4,128,1024]{2,1,0:T(8,128)(2,1)}), bf16[4,128,1024]{2,1,0:T(8,128)(2,1)S(1)}, u32[]{:S(2)}, u32[]{:S(2)}) async-start(bf16[4,128,1024]{2,1,0:T(8,128)(2,1)} %bitcast.68), calls=%async_computation | async-start | bytes 2097152 | tf_op jit(solution)/shard_map/all_to_all | solution.py:49
  42.8 468.5 %all-gather.14.cloned.1.call-start = ((), (), s32[]{:S(2)}) async-start(), calls=%async_computation.6 | async-start | bytes 1310720 | tf_op jit(solution)/shard_map/all_gather | solution.py:131
  56.3 1.0 copy-start.1
  209.4 1.0 copy-start.3
  209.4 0.9 copy-start.4
  210.3 1.0 copy-start.2
  212.0 16.0 %collective-permute-start = (bf16[512,512]{0,1:T(8,128)(2,1)}, bf16[512,512]{0,1:T(8,128)(2,1)S(1)}, u32[]{:S(2)}, u32[]{:S(2)}) collective-permute-start(bf16[512,512]{0,1:T(8,128)(2,1)} %get-tuple-element.353), channel_id=1, source_target_pairs={{0,16},{16,32},{32,48},{48,64},{64,80},{80,96},{96,112},{112,128},... | collective-permute-start | bytes 1572872 | tf_op jit(solution)/shard_map/while/body/eval_jaxpr/ppermute | solution.py:16
  228.8 17.7 %collective-permute-start = (bf16[512,512]{0,1:T(8,128)(2,1)}, bf16[512,512]{0,1:T(8,128)(2,1)S(1)}, u32[]{:S(2)}, u32[]{:S(2)}) collective-permute-start(bf16[512,512]{0,1:T(8,128)(2,1)} %get-tuple-element.353), channel_id=1, source_target_pairs={{0,16},{16,32},{32,48},{48,64},{64,80},{80,96},{96,112},{112,128},... | collective-permute-start | bytes 1572872 | tf_op jit(solution)/shard_map/while/body/eval_jaxpr/ppermute | solution.py:16
  247.3 15.2 %collective-permute-start = (bf16[512,512]{0,1:T(8,128)(2,1)}, bf16[512,512]{0,1:T(8,128)(2,1)S(1)}, u32[]{:S(2)}, u32[]{:S(2)}) collective-permute-start(bf16[512,512]{0,1:T(8,128)(2,1)} %get-tuple-element.353), channel_id=1, source_target_pairs={{0,16},{16,32},{32,48},{48,64},{64,80},{80,96},{96,112},{112,128},... | collective-permute-start | bytes 1572872 | tf_op jit(solution)/shard_map/while/body/eval_jaxpr/ppermute | solution.py:16
  263.3 15.2 %collective-permute-start = (bf16[512,512]{0,1:T(8,128)(2,1)}, bf16[512,512]{0,1:T(8,128)(2,1)S(1)}, u32[]{:S(2)}, u32[]{:S(2)}) collective-permute-start(bf16[512,512]{0,1:T(8,128)(2,1)} %get-tuple-element.353), channel_id=1, source_target_pairs={{0,16},{16,32},{32,48},{48,64},{64,80},{80,96},{96,112},{112,128},... | collective-permute-start | bytes 1572872 | tf_op jit(solution)/shard_map/while/body/eval_jaxpr/ppermute | solution.py:16
  279.3 14.3 %collective-permute-start = (bf16[512,512]{0,1:T(8,128)(2,1)}, bf16[512,512]{0,1:T(8,128)(2,1)S(1)}, u32[]{:S(2)}, u32[]{:S(2)}) collective-permute-start(bf16[512,512]{0,1:T(8,128)(2,1)} %get-tuple-element.353), channel_id=1, source_target_pairs={{0,16},{16,32},{32,48},{48,64},{64,80},{80,96},{96,112},{112,128},... | collective-permute-start | bytes 1572872 | tf_op jit(solution)/shard_map/while/body/eval_jaxpr/ppermute | solution.py:16
  294.3 15.5 %collective-permute-start = (bf16[512,512]{0,1:T(8,128)(2,1)}, bf16[512,512]{0,1:T(8,128)(2,1)S(1)}, u32[]{:S(2)}, u32[]{:S(2)}) collective-permute-start(bf16[512,512]{0,1:T(8,128)(2,1)} %get-tuple-element.353), channel_id=1, source_target_pairs={{0,16},{16,32},{32,48},{48,64},{64,80},{80,96},{96,112},{112,128},... | collective-permute-start | bytes 1572872 | tf_op jit(solution)/shard_map/while/body/eval_jaxpr/ppermute | solution.py:16
  310.6 13.0 %collective-permute-start = (bf16[512,512]{0,1:T(8,128)(2,1)}, bf16[512,512]{0,1:T(8,128)(2,1)S(1)}, u32[]{:S(2)}, u32[]{:S(2)}) collective-permute-start(bf16[512,512]{0,1:T(8,128)(2,1)} %get-tuple-element.353), channel_id=1, source_target_pairs={{0,16},{16,32},{32,48},{48,64},{64,80},{80,96},{96,112},{112,128},... | collective-permute-start | bytes 1572872 | tf_op jit(solution)/shard_map/while/body/eval_jaxpr/ppermute | solution.py:16
  324.4 14.2 %collective-permute-start = (bf16[512,512]{0,1:T(8,128)(2,1)}, bf16[512,512]{0,1:T(8,128)(2,1)S(1)}, u32[]{:S(2)}, u32[]{:S(2)}) collective-permute-start(bf16[512,512]{0,1:T(8,128)(2,1)} %get-tuple-element.353), channel_id=1, source_target_pairs={{0,16},{16,32},{32,48},{48,64},{64,80},{80,96},{96,112},{112,128},... | collective-permute-start | bytes 1572872 | tf_op jit(solution)/shard_map/while/body/eval_jaxpr/ppermute | solution.py:16
  339.4 12.5 %collective-permute-start = (bf16[512,512]{0,1:T(8,128)(2,1)}, bf16[512,512]{0,1:T(8,128)(2,1)S(1)}, u32[]{:S(2)}, u32[]{:S(2)}) collective-permute-start(bf16[512,512]{0,1:T(8,128)(2,1)} %get-tuple-element.353), channel_id=1, source_target_pairs={{0,16},{16,32},{32,48},{48,64},{64,80},{80,96},{96,112},{112,128},... | collective-permute-start | bytes 1572872 | tf_op jit(solution)/shard_map/while/body/eval_jaxpr/ppermute | solution.py:16
  352.7 13.4 %collective-permute-start = (bf16[512,512]{0,1:T(8,128)(2,1)}, bf16[512,512]{0,1:T(8,128)(2,1)S(1)}, u32[]{:S(2)}, u32[]{:S(2)}) collective-permute-start(bf16[512,512]{0,1:T(8,128)(2,1)} %get-tuple-element.353), channel_id=1, source_target_pairs={{0,16},{16,32},{32,48},{48,64},{64,80},{80,96},{96,112},{112,128},... | collective-permute-start | bytes 1572872 | tf_op jit(solution)/shard_map/while/body/eval_jaxpr/ppermute | solution.py:16
  366.9 11.6 %collective-permute-start = (bf16[512,512]{0,1:T(8,128)(2,1)}, bf16[512,512]{0,1:T(8,128)(2,1)S(1)}, u32[]{:S(2)}, u32[]{:S(2)}) collective-permute-start(bf16[512,512]{0,1:T(8,128)(2,1)} %get-tuple-element.353), channel_id=1, source_target_pairs={{0,16},{16,32},{32,48},{48,64},{64,80},{80,96},{96,112},{112,128},... | collective-permute-start | bytes 1572872 | tf_op jit(solution)/shard_map/while/body/eval_jaxpr/ppermute | solution.py:16
  379.3 14.8 %collective-permute-start = (bf16[512,512]{0,1:T(8,128)(2,1)}, bf16[512,512]{0,1:T(8,128)(2,1)S(1)}, u32[]{:S(2)}, u32[]{:S(2)}) collective-permute-start(bf16[512,512]{0,1:T(8,128)(2,1)} %get-tuple-element.353), channel_id=1, source_target_pairs={{0,16},{16,32},{32,48},{48,64},{64,80},{80,96},{96,112},{112,128},... | collective-permute-start | bytes 1572872 | tf_op jit(solution)/shard_map/while/body/eval_jaxpr/ppermute | solution.py:16
  394.9 14.7 %collective-permute-start = (bf16[512,512]{0,1:T(8,128)(2,1)}, bf16[512,512]{0,1:T(8,128)(2,1)S(1)}, u32[]{:S(2)}, u32[]{:S(2)}) collective-permute-start(bf16[512,512]{0,1:T(8,128)(2,1)} %get-tuple-element.353), channel_id=1, source_target_pairs={{0,16},{16,32},{32,48},{48,64},{64,80},{80,96},{96,112},{112,128},... | collective-permute-start | bytes 1572872 | tf_op jit(solution)/shard_map/while/body/eval_jaxpr/ppermute | solution.py:16
  410.4 19.5 %collective-permute-start = (bf16[512,512]{0,1:T(8,128)(2,1)}, bf16[512,512]{0,1:T(8,128)(2,1)S(1)}, u32[]{:S(2)}, u32[]{:S(2)}) collective-permute-start(bf16[512,512]{0,1:T(8,128)(2,1)} %get-tuple-element.353), channel_id=1, source_target_pairs={{0,16},{16,32},{32,48},{48,64},{64,80},{80,96},{96,112},{112,128},... | collective-permute-start | bytes 1572872 | tf_op jit(solution)/shard_map/while/body/eval_jaxpr/ppermute | solution.py:16
  430.7 12.4 %collective-permute-start = (bf16[512,512]{0,1:T(8,128)(2,1)}, bf16[512,512]{0,1:T(8,128)(2,1)S(1)}, u32[]{:S(2)}, u32[]{:S(2)}) collective-permute-start(bf16[512,512]{0,1:T(8,128)(2,1)} %get-tuple-element.353), channel_id=1, source_target_pairs={{0,16},{16,32},{32,48},{48,64},{64,80},{80,96},{96,112},{112,128},... | collective-permute-start | bytes 1572872 | tf_op jit(solution)/shard_map/while/body/eval_jaxpr/ppermute | solution.py:16
  444.9 98.2 %reduce-scatter.2.cloned.1.call-start = ((), (), s32[]{:S(2)}) async-start(), calls=%async_computation.7 | async-start | bytes 1310720 | tf_op jit(solution)/shard_map/reduce_scatter | solution.py:132
Sparse Core Ops, SparseCore 0:
  9.1 29.6 all-gather.5
  40.6 31.6 all-gather.7
  74.1 31.3 all-gather.9
  107.2 84.8 all-gather.11
  445.0 66.3 all-gather.13
  515.0 28.0 reduce-scatter.1
where the time goes:
time: 551 us; the launch traced here: 550 us
  waiting for transfers between devices  373 us (68%)
  starting transfers between devices  95.4 us (17%)
  local copies, waits for them, and re-layouts  42.2 us (8%)
  matrix products  14.9 us (3%)
  between operations  13.6 us (2%)
  blocking collectives  8.21 us (1%)
    ppermute x15, waiting for transfers between devices, passed_along(): lax.ppermute(value, axis, [(source, source + steps) for source in range(i...  128 us
    ppermute x15, starting transfers between devices, passed_along(): lax.ppermute(value, axis, [(source, source + steps) for source in range(i...  91.2 us
    all_gather x1, waiting for transfers between devices, on_device(): lax.all_gather(w_query, 'row', axis=0, tiled=True)  69.7 us
    all_gather x1, waiting for transfers between devices, on_device(): heads_block = lax.all_gather(heads_out, 'row', axis=0, tiled=True)  66.5 us
    all_gather x1, waiting for transfers between devices, on_device(): gathered_block = lax.all_gather(tokens, 'col', axis=0, tiled=True)  29.5 us
    reduce_scatter x1, waiting for transfers between devices, on_device(): lax.psum_scatter(jnp.dot(heads_block, w_output, preferred_element_type=jn...  28.2 us
    all_gather x1, waiting for transfers between devices, on_device(): lax.all_gather(w_value, 'row', axis=0, tiled=True)  26.6 us
    all_to_all x1, waiting for transfers between devices, on_device(): lax.all_to_all(gathered_block, 'row', split_axis=0, concat_axis=1, tiled=...  12.4 us
  transfers between devices with their start and end apart: 22, of which 22 were waited for; matrix products, arithmetic and copies ran while one was open for 4% of the time, Pallas kernels for 0%

commit v1 on v0

--- a/solution.py
+++ b/solution.py
@@ -8,6 +8,28 @@
 HEAD_DIM = 128
 rope_base = 500000.0
 masked_score = -1e30
+
+
+def laid_out(blocks, dim):
+    blocks = jnp.moveaxis(blocks, 0, dim)
+    lengths = blocks.shape
+    return blocks.reshape(*lengths[:dim], lengths[dim] * lengths[dim + 1], *lengths[dim + 2 :])
+
+
+def ring_gather(value, axis, dim):
+    size = lax.axis_size(axis)
+    pairs = [(i, (i + 1) % size) for i in range(size)]
+    back = [(b, a) for a, b in pairs]
+    lower, upper = ([], [])
+    for step in range(size - 1):
+        if step % 2 == 0:
+            lower.append(lax.ppermute(lower[-1] if lower else value, axis, pairs))
+        else:
+            upper.append(lax.ppermute(upper[-1] if upper else value, axis, back))
+    tiles = jnp.stack([*lower[::-1], value, *upper])
+    shift = lax.axis_index(axis) - len(lower)
+    tiles = tiles[(jnp.arange(size) - shift) % size]
+    return laid_out(tiles, dim)
 
 
 def passed_along(value, axis, steps):
@@ -44,7 +66,7 @@
     group = HEADS // KV_HEADS
     score_scale = HEAD_DIM ** (-0.5)
     local_index = jnp.arange(block_len, dtype=jnp.int32)
-    gathered_block = lax.all_gather(tokens, "col", axis=0, tiled=True)
+    gathered_block = ring_gather(tokens, "col", 0)
     block_pos = seq_at * block_len + local_index
     regrouped = lax.all_to_all(gathered_block, "row", split_axis=0, concat_axis=1, tiled=True)
     projected = jnp.concatenate(

time: 551 us -> 530 us (0.962)
  waiting for transfers between devices: 373 us -> 344 us
    all_gather x1 -> x0, waiting for transfers between devices: 29.5 us -> none  [on_device(): gathered_block = lax.all_gather(tokens, 'col', axis=0, tiled=True)]
    ppermute x0 -> x3, waiting for transfers between devices: none -> 14.2 us  [the longest x2 14.2 us: ring_gather(): lower.append(lax.ppermute(lower[-1] if lower else value, axis, pairs))]
    all_gather x1, waiting for transfers between devices: 26.6 us -> 16.8 us  [on_device(): lax.all_gather(w_value, 'row', axis=0, tiled=True)]
    all_gather x1, waiting for transfers between devices: 8.99 us -> 0.01 us  [on_device(): lax.all_gather(w_key, 'row', axis=0, tiled=True)]
    all_to_all x1, waiting for transfers between devices: 12.4 us -> 19.1 us  [on_device(): lax.all_to_all(gathered_block, 'row', split_axis=0, concat_axis=1, tiled=...]
  transfers between devices with their start and end apart: 22 -> 24, of which waited for: 22 -> 22; matrix products, arithmetic and copies ran while one was open for 4% -> 5% of each run, Pallas kernels for 0% -> 0%
where the time goes in v1:
time: 530 us; the launch traced here: 529 us
  waiting for transfers between devices  344 us (65%)
  starting transfers between devices  98.6 us (19%)
  local copies, waits for them, and re-layouts  45.3 us (9%)
  matrix products  15 us (3%)
  between operations  13.3 us (3%)
  blocking collectives  8.4 us (2%)
    ppermute x15, waiting for transfers between devices, passed_along(): lax.ppermute(value, axis, [(source, source + steps) for source in range(i...  128 us
    ppermute x15, starting transfers between devices, passed_along(): lax.ppermute(value, axis, [(source, source + steps) for source in range(i...  91.4 us
    all_gather x1, waiting for transfers between devices, on_device(): lax.all_gather(w_query, 'row', axis=0, tiled=True)  69.5 us
    all_gather x1, waiting for transfers between devices, on_device(): heads_block = lax.all_gather(heads_out, 'row', axis=0, tiled=True)  66.1 us
    reduce_scatter x1, waiting for transfers between devices, on_device(): lax.psum_scatter(jnp.dot(heads_block, w_output, preferred_element_type=jn...  28.2 us
    all_to_all x1, waiting for transfers between devices, on_device(): lax.all_to_all(gathered_block, 'row', split_axis=0, concat_axis=1, tiled=...  19.1 us
    all_gather x1, waiting for transfers between devices, on_device(): lax.all_gather(w_value, 'row', axis=0, tiled=True)  16.8 us
    ppermute x2, waiting for transfers between devices, ring_gather(): lower.append(lax.ppermute(lower[-1] if lower else value, axis, pairs))  14.2 us
  transfers between devices with their start and end apart: 24, of which 22 were waited for; matrix products, arithmetic and copies ran while one was open for 5% of the time, Pallas kernels for 0%

profile of v1, /device:TPU:2, one launch (start us, length us, event | category | flops | bytes accessed | tf_op | source)
XLA Modules:
  0.0 529.0 jit_solution(1086600263759001113)
XLA Ops:
  12.1 6.1 %collective-permute-done.1 = bf16[128,1024]{1,0:T(8,128)(2,1)S(1)} collective-permute-done((bf16[128,1024]{1,0:T(8,128)(2,1)S(1)}, bf16[128,1024]{1,0:T(8,128)(2,1)S(1)}, u32[]{:S(2)}, u32[]{:S(2)}) %collective-permute-start.1) | collective-permute-done | bytes 262176 | tf_op jit(solution)/shard_map/ppermute | solution.py:26
  18.5 8.1 %collective-permute-done.2 = bf16[128,1024]{1,0:T(8,128)(2,1)S(1)} collective-permute-done((bf16[128,1024]{1,0:T(8,128)(2,1)S(1)}, bf16[128,1024]{1,0:T(8,128)(2,1)S(1)}, u32[]{:S(2)}, u32[]{:S(2)}) %collective-permute-start.2) | collective-permute-done | bytes 262176 | tf_op jit(solution)/shard_map/ppermute | solution.py:26
  30.2 3.5 all-to-all-start
  34.8 19.1 %all-to-all-done = bf16[4,128,1024]{2,1,0:T(8,128)(2,1)S(1)} async-done(((bf16[4,128,1024]{2,1,0:T(8,128)(2,1)}), bf16[4,128,1024]{2,1,0:T(8,128)(2,1)S(1)}, u32[]{:S(2)}, u32[]{:S(2)}) %all-to-all-start) | async-done | bytes 1048608 | tf_op jit(solution)/shard_map/all_to_all | solution.py:71
  58.6 2.3 copy.45
  60.9 4.1 copy.20
  65.0 2.4 fusion.24
  67.6 16.8 %all-gather.7.cloned.1.call-done = bf16[4096,256]{1,0:T(8,128)(2,1)} async-done(((bf16[1024,256]{1,0:T(8,128)(2,1)}), bf16[4096,256]{1,0:T(8,128)(2,1)}) %all-gather.7.cloned.1.call-update) | async-done | bytes 2097168 | tf_op jit(solution)/shard_map/all_gather | solution.py:86
  84.4 2.4 convolution_convert_fusion.1
  86.8 8.4 %all_gather.17 = bf16[512,512]{1,0:T(8,128)(2,1)} all-gather(bf16[128,512]{1,0:T(8,128)(2,1)S(1)} %pad_maximum_fusion.1), channel_id=1, replica_groups=mesh['seq'=16,'row'=4,'col'=4] {'row'}, dimensions={0}, use_global_device_ids=true | all-gather | bytes 655360 | tf_op jit(solution)/shard_map/all_gather | solution.py:142
  95.2 2.1 copy.27
  101.6 69.5 %all-gather.9.cloned.1.call-done = bf16[4096,1024]{1,0:T(8,128)(2,1)} async-done(((bf16[1024,1024]{1,0:T(8,128)(2,1)}), bf16[4096,1024]{1,0:T(8,128)(2,1)}) %all-gather.9.cloned.1.call-update) | async-done | bytes 8388624 | tf_op jit(solution)/shard_map/all_gather | solution.py:76
  171.1 11.8 %copy.22 = bf16[1024,4096]{1,0:T(8,128)(2,1)} copy(bf16[1024,4096]{0,1:T(8,128)(2,1)} %bitcast.65) | data formatting | bytes 16777216 | tf_op jit(solution)/shard_map/dot_general | solution.py:74
  183.0 5.7 %fusion.25 = f32[128,8,128]{0,2,1:T(8,128)S(1)} fusion(bf16[128,4096,1]{1,0,2:T(8,128)(2,1)S(1)} %reshape.118, bf16[8,128,4096]{2,1,0:T(8,128)(2,1)} %bitcast.60), kind=kOutput, calls=%fused_computation.55 | convolution fusion | flops 1073741824 | bytes 9961472 | tf_op jit(solution)/shard_map/dot_general | solution.py:74
  191.2 232.4 %while.21 = (s32[]{:T(128)}, f32[2,4,128]{2,1,0:T(4,128)S(1)}, f32[2,4,128]{2,1,0:T(4,128)S(1)}, f32[2,4,128,128]{3,2,1,0:T(8,128)S(1)}, bf16[512,512]{0,1:T(8,1...) while((s32[]{:T(128)}, f32[2,4,128]{2,1,0:T(4,128)S(1)}, ...), condition=%wide.region_7.8_spmd, body=%wide.region_2.7_spmd.sunk | while | flops 272893952 | bytes 12386684 | solution.py:150
  191.2 3.5 collective-permute-start
  194.7 12.5 %collective-permute-done = bf16[512,512]{0,1:T(8,128)(2,1)S(1)} collective-permute-done((bf16[512,512]{0,1:T(8,128)(2,1)}, bf16[512,512]{0,1:T(8,128)(2,1)S(1)}, u32[]{:S(2)}, u32[]{:S(2)}) %collective-permute-start) | collective-permute-done | bytes 524320 | tf_op jit(solution)/shard_map/while/body/eval_jaxpr/ppermute | solution.py:38
  208.1 6.0 %collective-permute-start = (bf16[512,512]{0,1:T(8,128)(2,1)}, bf16[512,512]{0,1:T(8,128)(2,1)S(1)}, u32[]{:S(2)}, u32[]{:S(2)}) collective-permute-start(bf16[512,512]{0,1:T(8,128)(2,1)} %get-tuple-element.346), channel_id=1, source_target_pairs={{0,16},{16,32},{32,48},{48,64},{64,80},{80,96},{96,112},{112,128},... | collective-permute-start | bytes 1572872 | tf_op jit(solution)/shard_map/while/body/eval_jaxpr/ppermute | solution.py:38
  214.1 11.7 %collective-permute-done = bf16[512,512]{0,1:T(8,128)(2,1)S(1)} collective-permute-done((bf16[512,512]{0,1:T(8,128)(2,1)}, bf16[512,512]{0,1:T(8,128)(2,1)S(1)}, u32[]{:S(2)}, u32[]{:S(2)}) %collective-permute-start) | collective-permute-done | bytes 524320 | tf_op jit(solution)/shard_map/while/body/eval_jaxpr/ppermute | solution.py:38
  226.6 4.3 collective-permute-start
  231.0 10.8 %collective-permute-done = bf16[512,512]{0,1:T(8,128)(2,1)S(1)} collective-permute-done((bf16[512,512]{0,1:T(8,128)(2,1)}, bf16[512,512]{0,1:T(8,128)(2,1)S(1)}, u32[]{:S(2)}, u32[]{:S(2)}) %collective-permute-start) | collective-permute-done | bytes 524320 | tf_op jit(solution)/shard_map/while/body/eval_jaxpr/ppermute | solution.py:38
  242.6 5.2 collective-permute-start
  247.8 10.0 %collective-permute-done = bf16[512,512]{0,1:T(8,128)(2,1)S(1)} collective-permute-done((bf16[512,512]{0,1:T(8,128)(2,1)}, bf16[512,512]{0,1:T(8,128)(2,1)S(1)}, u32[]{:S(2)}, u32[]{:S(2)}) %collective-permute-start) | collective-permute-done | bytes 524320 | tf_op jit(solution)/shard_map/while/body/eval_jaxpr/ppermute | solution.py:38
  258.7 5.1 collective-permute-start
  263.8 9.1 %collective-permute-done = bf16[512,512]{0,1:T(8,128)(2,1)S(1)} collective-permute-done((bf16[512,512]{0,1:T(8,128)(2,1)}, bf16[512,512]{0,1:T(8,128)(2,1)S(1)}, u32[]{:S(2)}, u32[]{:S(2)}) %collective-permute-start) | collective-permute-done | bytes 524320 | tf_op jit(solution)/shard_map/while/body/eval_jaxpr/ppermute | solution.py:38
  273.7 7.2 %collective-permute-start = (bf16[512,512]{0,1:T(8,128)(2,1)}, bf16[512,512]{0,1:T(8,128)(2,1)S(1)}, u32[]{:S(2)}, u32[]{:S(2)}) collective-permute-start(bf16[512,512]{0,1:T(8,128)(2,1)} %get-tuple-element.346), channel_id=1, source_target_pairs={{0,16},{16,32},{32,48},{48,64},{64,80},{80,96},{96,112},{112,128},... | collective-permute-start | bytes 1572872 | tf_op jit(solution)/shard_map/while/body/eval_jaxpr/ppermute | solution.py:38
  281.0 8.3 %collective-permute-done = bf16[512,512]{0,1:T(8,128)(2,1)S(1)} collective-permute-done((bf16[512,512]{0,1:T(8,128)(2,1)}, bf16[512,512]{0,1:T(8,128)(2,1)S(1)}, u32[]{:S(2)}, u32[]{:S(2)}) %collective-permute-start) | collective-permute-done | bytes 524320 | tf_op jit(solution)/shard_map/while/body/eval_jaxpr/ppermute | solution.py:38
  290.1 5.5 %collective-permute-start = (bf16[512,512]{0,1:T(8,128)(2,1)}, bf16[512,512]{0,1:T(8,128)(2,1)S(1)}, u32[]{:S(2)}, u32[]{:S(2)}) collective-permute-start(bf16[512,512]{0,1:T(8,128)(2,1)} %get-tuple-element.346), channel_id=1, source_target_pairs={{0,16},{16,32},{32,48},{48,64},{64,80},{80,96},{96,112},{112,128},... | collective-permute-start | bytes 1572872 | tf_op jit(solution)/shard_map/while/body/eval_jaxpr/ppermute | solution.py:38
  295.7 7.4 %collective-permute-done = bf16[512,512]{0,1:T(8,128)(2,1)S(1)} collective-permute-done((bf16[512,512]{0,1:T(8,128)(2,1)}, bf16[512,512]{0,1:T(8,128)(2,1)S(1)}, u32[]{:S(2)}, u32[]{:S(2)}) %collective-permute-start) | collective-permute-done | bytes 524320 | tf_op jit(solution)/shard_map/while/body/eval_jaxpr/ppermute | solution.py:38
  303.9 7.2 %collective-permute-start = (bf16[512,512]{0,1:T(8,128)(2,1)}, bf16[512,512]{0,1:T(8,128)(2,1)S(1)}, u32[]{:S(2)}, u32[]{:S(2)}) collective-permute-start(bf16[512,512]{0,1:T(8,128)(2,1)} %get-tuple-element.346), channel_id=1, source_target_pairs={{0,16},{16,32},{32,48},{48,64},{64,80},{80,96},{96,112},{112,128},... | collective-permute-start | bytes 1572872 | tf_op jit(solution)/shard_map/while/body/eval_jaxpr/ppermute | solution.py:38
  311.2 6.9 %collective-permute-done = bf16[512,512]{0,1:T(8,128)(2,1)S(1)} collective-permute-done((bf16[512,512]{0,1:T(8,128)(2,1)}, bf16[512,512]{0,1:T(8,128)(2,1)S(1)}, u32[]{:S(2)}, u32[]{:S(2)}) %collective-permute-start) | collective-permute-done | bytes 524320 | tf_op jit(solution)/shard_map/while/body/eval_jaxpr/ppermute | solution.py:38
  319.0 5.5 %collective-permute-start = (bf16[512,512]{0,1:T(8,128)(2,1)}, bf16[512,512]{0,1:T(8,128)(2,1)S(1)}, u32[]{:S(2)}, u32[]{:S(2)}) collective-permute-start(bf16[512,512]{0,1:T(8,128)(2,1)} %get-tuple-element.346), channel_id=1, source_target_pairs={{0,16},{16,32},{32,48},{48,64},{64,80},{80,96},{96,112},{112,128},... | collective-permute-start | bytes 1572872 | tf_op jit(solution)/shard_map/while/body/eval_jaxpr/ppermute | solution.py:38
  324.5 6.9 %collective-permute-done = bf16[512,512]{0,1:T(8,128)(2,1)S(1)} collective-permute-done((bf16[512,512]{0,1:T(8,128)(2,1)}, bf16[512,512]{0,1:T(8,128)(2,1)S(1)}, u32[]{:S(2)}, u32[]{:S(2)}) %collective-permute-start) | collective-permute-done | bytes 524320 | tf_op jit(solution)/shard_map/while/body/eval_jaxpr/ppermute | solution.py:38
  332.3 5.5 %collective-permute-start = (bf16[512,512]{0,1:T(8,128)(2,1)}, bf16[512,512]{0,1:T(8,128)(2,1)S(1)}, u32[]{:S(2)}, u32[]{:S(2)}) collective-permute-start(bf16[512,512]{0,1:T(8,128)(2,1)} %get-tuple-element.346), channel_id=1, source_target_pairs={{0,16},{16,32},{32,48},{48,64},{64,80},{80,96},{96,112},{112,128},... | collective-permute-start | bytes 1572872 | tf_op jit(solution)/shard_map/while/body/eval_jaxpr/ppermute | solution.py:38
  337.8 7.8 %collective-permute-done = bf16[512,512]{0,1:T(8,128)(2,1)S(1)} collective-permute-done((bf16[512,512]{0,1:T(8,128)(2,1)}, bf16[512,512]{0,1:T(8,128)(2,1)S(1)}, u32[]{:S(2)}, u32[]{:S(2)}) %collective-permute-start) | collective-permute-done | bytes 524320 | tf_op jit(solution)/shard_map/while/body/eval_jaxpr/ppermute | solution.py:38
  346.4 4.7 collective-permute-start
  351.1 6.9 %collective-permute-done = bf16[512,512]{0,1:T(8,128)(2,1)S(1)} collective-permute-done((bf16[512,512]{0,1:T(8,128)(2,1)}, bf16[512,512]{0,1:T(8,128)(2,1)S(1)}, u32[]{:S(2)}, u32[]{:S(2)}) %collective-permute-start) | collective-permute-done | bytes 524320 | tf_op jit(solution)/shard_map/while/body/eval_jaxpr/ppermute | solution.py:38
  358.9 7.7 %collective-permute-start = (bf16[512,512]{0,1:T(8,128)(2,1)}, bf16[512,512]{0,1:T(8,128)(2,1)S(1)}, u32[]{:S(2)}, u32[]{:S(2)}) collective-permute-start(bf16[512,512]{0,1:T(8,128)(2,1)} %get-tuple-element.346), channel_id=1, source_target_pairs={{0,16},{16,32},{32,48},{48,64},{64,80},{80,96},{96,112},{112,128},... | collective-permute-start | bytes 1572872 | tf_op jit(solution)/shard_map/while/body/eval_jaxpr/ppermute | solution.py:38
  366.6 7.1 %collective-permute-done = bf16[512,512]{0,1:T(8,128)(2,1)S(1)} collective-permute-done((bf16[512,512]{0,1:T(8,128)(2,1)}, bf16[512,512]{0,1:T(8,128)(2,1)S(1)}, u32[]{:S(2)}, u32[]{:S(2)}) %collective-permute-start) | collective-permute-done | bytes 524320 | tf_op jit(solution)/shard_map/while/body/eval_jaxpr/ppermute | solution.py:38
  374.5 7.8 %collective-permute-start = (bf16[512,512]{0,1:T(8,128)(2,1)}, bf16[512,512]{0,1:T(8,128)(2,1)S(1)}, u32[]{:S(2)}, u32[]{:S(2)}) collective-permute-start(bf16[512,512]{0,1:T(8,128)(2,1)} %get-tuple-element.346), channel_id=1, source_target_pairs={{0,16},{16,32},{32,48},{48,64},{64,80},{80,96},{96,112},{112,128},... | collective-permute-start | bytes 1572872 | tf_op jit(solution)/shard_map/while/body/eval_jaxpr/ppermute | solution.py:38
  382.3 6.9 %collective-permute-done = bf16[512,512]{0,1:T(8,128)(2,1)S(1)} collective-permute-done((bf16[512,512]{0,1:T(8,128)(2,1)}, bf16[512,512]{0,1:T(8,128)(2,1)S(1)}, u32[]{:S(2)}, u32[]{:S(2)}) %collective-permute-start) | collective-permute-done | bytes 524320 | tf_op jit(solution)/shard_map/while/body/eval_jaxpr/ppermute | solution.py:38
  390.1 10.7 %collective-permute-start = (bf16[512,512]{0,1:T(8,128)(2,1)}, bf16[512,512]{0,1:T(8,128)(2,1)S(1)}, u32[]{:S(2)}, u32[]{:S(2)}) collective-permute-start(bf16[512,512]{0,1:T(8,128)(2,1)} %get-tuple-element.346), channel_id=1, source_target_pairs={{0,16},{16,32},{32,48},{48,64},{64,80},{80,96},{96,112},{112,128},... | collective-permute-start | bytes 1572872 | tf_op jit(solution)/shard_map/while/body/eval_jaxpr/ppermute | solution.py:38
  400.8 8.7 %collective-permute-done = bf16[512,512]{0,1:T(8,128)(2,1)S(1)} collective-permute-done((bf16[512,512]{0,1:T(8,128)(2,1)}, bf16[512,512]{0,1:T(8,128)(2,1)S(1)}, u32[]{:S(2)}, u32[]{:S(2)}) %collective-permute-start) | collective-permute-done | bytes 524320 | tf_op jit(solution)/shard_map/while/body/eval_jaxpr/ppermute | solution.py:38
  410.4 5.5 %collective-permute-start = (bf16[512,512]{0,1:T(8,128)(2,1)}, bf16[512,512]{0,1:T(8,128)(2,1)S(1)}, u32[]{:S(2)}, u32[]{:S(2)}) collective-permute-start(bf16[512,512]{0,1:T(8,128)(2,1)} %get-tuple-element.346), channel_id=1, source_target_pairs={{0,16},{16,32},{32,48},{48,64},{64,80},{80,96},{96,112},{112,128},... | collective-permute-start | bytes 1572872 | tf_op jit(solution)/shard_map/while/body/eval_jaxpr/ppermute | solution.py:38
  415.9 6.9 %collective-permute-done = bf16[512,512]{0,1:T(8,128)(2,1)S(1)} collective-permute-done((bf16[512,512]{0,1:T(8,128)(2,1)}, bf16[512,512]{0,1:T(8,128)(2,1)S(1)}, u32[]{:S(2)}, u32[]{:S(2)}) %collective-permute-start) | collective-permute-done | bytes 524320 | tf_op jit(solution)/shard_map/while/body/eval_jaxpr/ppermute | solution.py:38
  424.7 66.1 %all-gather.11.cloned.1.call-done = bf16[512,1024]{0,1:T(8,128)(2,1)} async-done(((bf16[128,1024]{0,1:T(8,128)(2,1)}), bf16[512,1024]{0,1:T(8,128)(2,1)}) %all-gather.11.cloned.1.call-update) | async-done | bytes 1048592 | tf_op jit(solution)/shard_map/all_gather | solution.py:153
  490.8 3.5 convolution_convert_fusion
  494.3 28.2 %reduce-scatter.2.cloned.1.call-done = bf16[128,1024]{1,0:T(8,128)(2,1)} async-done(((bf16[512,1024]{1,0:T(8,128)(2,1)}), bf16[128,1024]{1,0:T(8,128)(2,1)}) %reduce-scatter.2.cloned.1.call-update) | async-done | bytes 262160 | tf_op jit(solution)/shard_map/reduce_scatter | solution.py:154
  (92 shorter events, 35.5 us)
Async XLA Ops:
  6.5 484.3 %copy-start = (bf16[1024,1024]{1,0:T(8,128)(2,1)S(1)}, bf16[1024,1024]{1,0:T(8,128)(2,1)}, u32[]{:S(2)}) copy-start(bf16[1024,1024]{1,0:T(8,128)(2,1)} %param.13) | copy-start | bytes 6291460
  6.5 2.2 copy-start.4
  6.5 54.4 %all-gather.5.cloned.1.call-start = ((), (), s32[]{:S(2)}) async-start(), calls=%async_computation.2 | async-start | bytes 2621440 | tf_op jit(solution)/shard_map/all_gather | solution.py:81
  7.3 77.2 %all-gather.7.cloned.1.call-start = ((), (), s32[]{:S(2)}) async-start(), calls=%async_computation.3 | async-start | bytes 2621440 | tf_op jit(solution)/shard_map/all_gather | solution.py:86
  8.0 163.1 %all-gather.9.cloned.1.call-start = ((), (), s32[]{:S(2)}) async-start(), calls=%async_computation.4 | async-start | bytes 10485760 | tf_op jit(solution)/shard_map/all_gather | solution.py:76
  8.8 9.4 %collective-permute-start.1 = (bf16[128,1024]{1,0:T(8,128)(2,1)S(1)}, bf16[128,1024]{1,0:T(8,128)(2,1)S(1)}, u32[]{:S(2)}, u32[]{:S(2)}) collective-permute-start(bf16[128,1024]{1,0:T(8,128)(2,1)S(1)} %copy-done.4), channel_id=1, source_target_pairs={{0,1},{1,2},{2,3},{3,0},{4,5},{5,6},{6,7},{7,4},{8,9},{9,10},{10,1... | collective-permute-start | bytes 786440 | tf_op jit(solution)/shard_map/ppermute | solution.py:26
  10.4 8.1 %collective-permute-start.3 = (bf16[128,1024]{1,0:T(8,128)(2,1)S(1)}, bf16[128,1024]{1,0:T(8,128)(2,1)S(1)}, u32[]{:S(2)}, u32[]{:S(2)}) collective-permute-start(bf16[128,1024]{1,0:T(8,128)(2,1)S(1)} %copy-done.4), channel_id=1, source_target_pairs={{1,0},{2,1},{3,2},{0,3},{5,4},{6,5},{7,6},{4,7},{9,8},{10,9},{11,1... | collective-permute-start | bytes 786440 | tf_op jit(solution)/shard_map/ppermute | solution.py:28
  18.2 8.5 %copy-start.5 = (bf16[128,1024]{1,0:T(8,128)(2,1)}, bf16[128,1024]{1,0:T(8,128)(2,1)S(1)}, u32[]{:S(2)}) copy-start(bf16[128,1024]{1,0:T(8,128)(2,1)S(1)} %collective-permute-done.1) | copy-start | bytes 786436
  18.2 8.5 %collective-permute-start.2 = (bf16[128,1024]{1,0:T(8,128)(2,1)S(1)}, bf16[128,1024]{1,0:T(8,128)(2,1)S(1)}, u32[]{:S(2)}, u32[]{:S(2)}) collective-permute-start(bf16[128,1024]{1,0:T(8,128)(2,1)S(1)} %collective-permute-done.1), channel_id=1, source_target_pairs={{0,1},{1,2},{2,3},{3,0},{4,5},{5,6},{6,7},{7,4},{8,9},{9,10},{10,1... | collective-permute-start | bytes 786440 | tf_op jit(solution)/shard_map/ppermute | solution.py:26
  18.5 8.1 %copy-start.6 = (bf16[128,1024]{1,0:T(8,128)(2,1)}, bf16[128,1024]{1,0:T(8,128)(2,1)S(1)}, u32[]{:S(2)}) copy-start(bf16[128,1024]{1,0:T(8,128)(2,1)S(1)} %collective-permute-done.3) | copy-start | bytes 786436
  26.6 0.7 copy-start.7
  30.2 23.7 %all-to-all-start = ((bf16[4,128,1024]{2,1,0:T(8,128)(2,1)}), bf16[4,128,1024]{2,1,0:T(8,128)(2,1)S(1)}, u32[]{:S(2)}, u32[]{:S(2)}) async-start(bf16[4,128,1024]{2,1,0:T(8,128)(2,1)} %gather_fusion), calls=%async_computation | async-start | bytes 2097152 | tf_op jit(solution)/shard_map/all_to_all | solution.py:71
  33.7 457.1 %all-gather.11.cloned.1.call-start = ((), (), s32[]{:S(2)}) async-start(), calls=%async_computation.5 | async-start | bytes 1310720 | tf_op jit(solution)/shard_map/all_gather | solution.py:153
  54.0 1.0 copy-start.1
  188.7 1.0 copy-start.3
  188.7 0.9 copy-start.8
  189.6 1.0 copy-start.2
  191.2 16.0 %collective-permute-start = (bf16[512,512]{0,1:T(8,128)(2,1)}, bf16[512,512]{0,1:T(8,128)(2,1)S(1)}, u32[]{:S(2)}, u32[]{:S(2)}) collective-permute-start(bf16[512,512]{0,1:T(8,128)(2,1)} %get-tuple-element.346), channel_id=1, source_target_pairs={{0,16},{16,32},{32,48},{48,64},{64,80},{80,96},{96,112},{112,128},... | collective-permute-start | bytes 1572872 | tf_op jit(solution)/shard_map/while/body/eval_jaxpr/ppermute | solution.py:38
  208.1 17.7 %collective-permute-start = (bf16[512,512]{0,1:T(8,128)(2,1)}, bf16[512,512]{0,1:T(8,128)(2,1)S(1)}, u32[]{:S(2)}, u32[]{:S(2)}) collective-permute-start(bf16[512,512]{0,1:T(8,128)(2,1)} %get-tuple-element.346), channel_id=1, source_target_pairs={{0,16},{16,32},{32,48},{48,64},{64,80},{80,96},{96,112},{112,128},... | collective-permute-start | bytes 1572872 | tf_op jit(solution)/shard_map/while/body/eval_jaxpr/ppermute | solution.py:38
  226.6 15.2 %collective-permute-start = (bf16[512,512]{0,1:T(8,128)(2,1)}, bf16[512,512]{0,1:T(8,128)(2,1)S(1)}, u32[]{:S(2)}, u32[]{:S(2)}) collective-permute-start(bf16[512,512]{0,1:T(8,128)(2,1)} %get-tuple-element.346), channel_id=1, source_target_pairs={{0,16},{16,32},{32,48},{48,64},{64,80},{80,96},{96,112},{112,128},... | collective-permute-start | bytes 1572872 | tf_op jit(solution)/shard_map/while/body/eval_jaxpr/ppermute | solution.py:38
  242.6 15.2 %collective-permute-start = (bf16[512,512]{0,1:T(8,128)(2,1)}, bf16[512,512]{0,1:T(8,128)(2,1)S(1)}, u32[]{:S(2)}, u32[]{:S(2)}) collective-permute-start(bf16[512,512]{0,1:T(8,128)(2,1)} %get-tuple-element.346), channel_id=1, source_target_pairs={{0,16},{16,32},{32,48},{48,64},{64,80},{80,96},{96,112},{112,128},... | collective-permute-start | bytes 1572872 | tf_op jit(solution)/shard_map/while/body/eval_jaxpr/ppermute | solution.py:38
  258.7 14.3 %collective-permute-start = (bf16[512,512]{0,1:T(8,128)(2,1)}, bf16[512,512]{0,1:T(8,128)(2,1)S(1)}, u32[]{:S(2)}, u32[]{:S(2)}) collective-permute-start(bf16[512,512]{0,1:T(8,128)(2,1)} %get-tuple-element.346), channel_id=1, source_target_pairs={{0,16},{16,32},{32,48},{48,64},{64,80},{80,96},{96,112},{112,128},... | collective-permute-start | bytes 1572872 | tf_op jit(solution)/shard_map/while/body/eval_jaxpr/ppermute | solution.py:38
  273.7 15.5 %collective-permute-start = (bf16[512,512]{0,1:T(8,128)(2,1)}, bf16[512,512]{0,1:T(8,128)(2,1)S(1)}, u32[]{:S(2)}, u32[]{:S(2)}) collective-permute-start(bf16[512,512]{0,1:T(8,128)(2,1)} %get-tuple-element.346), channel_id=1, source_target_pairs={{0,16},{16,32},{32,48},{48,64},{64,80},{80,96},{96,112},{112,128},... | collective-permute-start | bytes 1572872 | tf_op jit(solution)/shard_map/while/body/eval_jaxpr/ppermute | solution.py:38
  290.1 13.0 %collective-permute-start = (bf16[512,512]{0,1:T(8,128)(2,1)}, bf16[512,512]{0,1:T(8,128)(2,1)S(1)}, u32[]{:S(2)}, u32[]{:S(2)}) collective-permute-start(bf16[512,512]{0,1:T(8,128)(2,1)} %get-tuple-element.346), channel_id=1, source_target_pairs={{0,16},{16,32},{32,48},{48,64},{64,80},{80,96},{96,112},{112,128},... | collective-permute-start | bytes 1572872 | tf_op jit(solution)/shard_map/while/body/eval_jaxpr/ppermute | solution.py:38
  303.9 14.2 %collective-permute-start = (bf16[512,512]{0,1:T(8,128)(2,1)}, bf16[512,512]{0,1:T(8,128)(2,1)S(1)}, u32[]{:S(2)}, u32[]{:S(2)}) collective-permute-start(bf16[512,512]{0,1:T(8,128)(2,1)} %get-tuple-element.346), channel_id=1, source_target_pairs={{0,16},{16,32},{32,48},{48,64},{64,80},{80,96},{96,112},{112,128},... | collective-permute-start | bytes 1572872 | tf_op jit(solution)/shard_map/while/body/eval_jaxpr/ppermute | solution.py:38
  319.0 12.5 %collective-permute-start = (bf16[512,512]{0,1:T(8,128)(2,1)}, bf16[512,512]{0,1:T(8,128)(2,1)S(1)}, u32[]{:S(2)}, u32[]{:S(2)}) collective-permute-start(bf16[512,512]{0,1:T(8,128)(2,1)} %get-tuple-element.346), channel_id=1, source_target_pairs={{0,16},{16,32},{32,48},{48,64},{64,80},{80,96},{96,112},{112,128},... | collective-permute-start | bytes 1572872 | tf_op jit(solution)/shard_map/while/body/eval_jaxpr/ppermute | solution.py:38
  332.3 13.3 %collective-permute-start = (bf16[512,512]{0,1:T(8,128)(2,1)}, bf16[512,512]{0,1:T(8,128)(2,1)S(1)}, u32[]{:S(2)}, u32[]{:S(2)}) collective-permute-start(bf16[512,512]{0,1:T(8,128)(2,1)} %get-tuple-element.346), channel_id=1, source_target_pairs={{0,16},{16,32},{32,48},{48,64},{64,80},{80,96},{96,112},{112,128},... | collective-permute-start | bytes 1572872 | tf_op jit(solution)/shard_map/while/body/eval_jaxpr/ppermute | solution.py:38
  346.4 11.6 %collective-permute-start = (bf16[512,512]{0,1:T(8,128)(2,1)}, bf16[512,512]{0,1:T(8,128)(2,1)S(1)}, u32[]{:S(2)}, u32[]{:S(2)}) collective-permute-start(bf16[512,512]{0,1:T(8,128)(2,1)} %get-tuple-element.346), channel_id=1, source_target_pairs={{0,16},{16,32},{32,48},{48,64},{64,80},{80,96},{96,112},{112,128},... | collective-permute-start | bytes 1572872 | tf_op jit(solution)/shard_map/while/body/eval_jaxpr/ppermute | solution.py:38
  358.9 14.8 %collective-permute-start = (bf16[512,512]{0,1:T(8,128)(2,1)}, bf16[512,512]{0,1:T(8,128)(2,1)S(1)}, u32[]{:S(2)}, u32[]{:S(2)}) collective-permute-start(bf16[512,512]{0,1:T(8,128)(2,1)} %get-tuple-element.346), channel_id=1, source_target_pairs={{0,16},{16,32},{32,48},{48,64},{64,80},{80,96},{96,112},{112,128},... | collective-permute-start | bytes 1572872 | tf_op jit(solution)/shard_map/while/body/eval_jaxpr/ppermute | solution.py:38
  374.5 14.8 %collective-permute-start = (bf16[512,512]{0,1:T(8,128)(2,1)}, bf16[512,512]{0,1:T(8,128)(2,1)S(1)}, u32[]{:S(2)}, u32[]{:S(2)}) collective-permute-start(bf16[512,512]{0,1:T(8,128)(2,1)} %get-tuple-element.346), channel_id=1, source_target_pairs={{0,16},{16,32},{32,48},{48,64},{64,80},{80,96},{96,112},{112,128},... | collective-permute-start | bytes 1572872 | tf_op jit(solution)/shard_map/while/body/eval_jaxpr/ppermute | solution.py:38
  390.1 19.4 %collective-permute-start = (bf16[512,512]{0,1:T(8,128)(2,1)}, bf16[512,512]{0,1:T(8,128)(2,1)S(1)}, u32[]{:S(2)}, u32[]{:S(2)}) collective-permute-start(bf16[512,512]{0,1:T(8,128)(2,1)} %get-tuple-element.346), channel_id=1, source_target_pairs={{0,16},{16,32},{32,48},{48,64},{64,80},{80,96},{96,112},{112,128},... | collective-permute-start | bytes 1572872 | tf_op jit(solution)/shard_map/while/body/eval_jaxpr/ppermute | solution.py:38
  410.4 12.4 %collective-permute-start = (bf16[512,512]{0,1:T(8,128)(2,1)}, bf16[512,512]{0,1:T(8,128)(2,1)S(1)}, u32[]{:S(2)}, u32[]{:S(2)}) collective-permute-start(bf16[512,512]{0,1:T(8,128)(2,1)} %get-tuple-element.346), channel_id=1, source_target_pairs={{0,16},{16,32},{32,48},{48,64},{64,80},{80,96},{96,112},{112,128},... | collective-permute-start | bytes 1572872 | tf_op jit(solution)/shard_map/while/body/eval_jaxpr/ppermute | solution.py:38
  424.6 97.8 %reduce-scatter.2.cloned.1.call-start = ((), (), s32[]{:S(2)}) async-start(), calls=%async_computation.6 | async-start | bytes 1310720 | tf_op jit(solution)/shard_map/reduce_scatter | solution.py:154
Sparse Core Ops, SparseCore 0:
  9.1 40.8 all-gather.4
  51.9 32.5 all-gather.6
  86.3 84.8 all-gather.8
  424.7 66.0 all-gather.10
  494.4 28.0 reduce-scatter.1
